TPU v7x, 128 devices: a whole 4x4x4 slice. The times are simulated.
128 devices in a mesh: dp: 8 (over x, core), tensor: 16 (over z, y).
Axes of the slice: x: 4, y: 4, z: 4, core: 2. Of those that a mesh axis runs over, the one named last changes fastest.
Arguments:
- hidden: bfloat16 [2048, 8192], P('dp', 'tensor'), may hold values from -170 to 170, as said below
- neighbour_ids: int32 [32, 2], P('dp'), may hold values from 0 to 255, as said below
- database: bfloat16 [256, 128, 8192], P('dp', None, 'tensor'), may hold values from -6 to 6
- w_query: bfloat16 [8192, 4096], P(None, 'tensor'), may hold values from -0.0625 to 0.0625
- w_key: bfloat16 [8192, 4096], P(None, 'tensor'), may hold values from -0.0625 to 0.0625
- w_value: bfloat16 [8192, 4096], P(None, 'tensor'), may hold values from -0.0625 to 0.0625
- w_out: bfloat16 [4096, 8192], P('tensor'), may hold values from -0.09375 to 0.09375
Outputs:
- mixed: bfloat16 [2048, 8192], P('dp', 'tensor')
Inputs may be any that keep to these rules, and one draw needn't show every extreme that they name: `neighbour_ids`: database block b is held by index b // 32 of dp. Among the 8 neighbour ids of one sequence (the rows of one device), at most 4 belong to the same holder, and in every sequence exactly 4 do. `hidden`: hidden states may be large for some tokens.
All inputs are finite; a program needn't handle non-finite values.
Results may differ from a plain program's by a relative error of at most 0.02.
Values may be sent and summed in bfloat16 or wider, within the bound.
No kernel may reach another device: no remote copies, remote signals or barrier semaphores. Data moves between devices by JAX's collectives and lax.ppermute only.
A program may use at most 128 MiB of HBM per device.

v0:
```python
import jax
import jax.numpy as jnp
from jax import lax
from jax.sharding import PartitionSpec as P

HD = 128


def attend(query_rows, key_rows, value_rows, heads_count, group_len):
    tok_count, width = query_rows.shape
    groups = tok_count // group_len
    head_size = width // heads_count
    shifted = jnp.concatenate(
        [query_rows[group_len - 1 :], jnp.zeros((group_len - 1, width), jnp.bfloat16)], 0
    )
    shifted = shifted.reshape(groups, group_len, heads_count, head_size)
    key_block = key_rows.reshape(groups, -1, heads_count, head_size)
    value_block = value_rows.reshape(groups, -1, heads_count, head_size)
    scores = jnp.einsum(
        "cqhd,ckhd->chqk", shifted, key_block, preferred_element_type=jnp.float32
    ) / jnp.sqrt(jnp.float32(head_size))
    top_score = jnp.max(scores, axis=-1, keepdims=True)
    weights_raw = jnp.exp(scores - top_score)
    soft = (weights_raw / jnp.sum(weights_raw, axis=-1, keepdims=True)).astype(jnp.bfloat16)
    blended = jnp.einsum(
        "chqk,ckhd->cqhd", soft, value_block, preferred_element_type=jnp.float32
    ).astype(jnp.bfloat16)
    blended = blended.reshape(tok_count, width)
    return jnp.concatenate(
        [jnp.zeros((group_len - 1, width), jnp.bfloat16), blended[: tok_count - group_len + 1]], 0
    )


def shards(hidden, neighbour_ids, database, w_query, w_key, w_value, w_out):
    dp_count = lax.axis_size("dp")
    tok_rows = hidden.shape[0]
    group_count = neighbour_ids.shape[0]
    per_reader = group_count * neighbour_ids.shape[1]
    capacity = per_reader // 2
    db_count = database.shape[0]
    ret_len = database.shape[1]
    col_count = database.shape[2]
    head_cols = w_query.shape[1]
    heads_local = head_cols // HD
    query_sum = jnp.dot(
        lax.all_gather(hidden, "tensor", axis=1, tiled=True),
        w_query,
        preferred_element_type=jnp.float32,
    )
    query_rows = query_sum.astype(jnp.bfloat16)
    block_ids = neighbour_ids.reshape(per_reader)
    owners = block_ids // db_count
    earlier = jnp.arange(per_reader)[:, None] > jnp.arange(per_reader)[None, :]
    slot_rank = jnp.sum(((owners[:, None] == owners[None, :]) & earlier).astype(jnp.int32), 1)
    slot_range = jnp.arange(capacity, dtype=jnp.int32)
    local_index = block_ids % db_count
    owner_range = jnp.arange(dp_count, dtype=jnp.int32)
    slot_hit = (owners[:, None, None] == owner_range[None, :, None]) & (
        slot_rank[:, None, None] == slot_range[None, None, :]
    )
    request_table = jnp.sum(slot_hit.astype(jnp.int32) * local_index[:, None, None], 0)
    requested = lax.all_to_all(request_table, "dp", split_axis=0, concat_axis=0, tiled=True)
    outgoing = jnp.take(database, requested.reshape(-1), axis=0).reshape(
        dp_count, capacity, ret_len, col_count
    )
    arrived = lax.all_to_all(outgoing, "dp", split_axis=0, concat_axis=0, tiled=True)
    neighbour_rows = jnp.take(
        arrived.reshape(dp_count * capacity, ret_len, col_count),
        owners * capacity + slot_rank,
        axis=0,
    )
    assembled = lax.all_gather(neighbour_rows, "tensor", axis=2, tiled=True).reshape(
        per_reader * ret_len, -1
    )
    key_sum = jnp.dot(assembled, w_key, preferred_element_type=jnp.float32)
    value_sum = jnp.dot(assembled, w_value, preferred_element_type=jnp.float32)
    key_rows = key_sum.astype(jnp.bfloat16)
    value_rows = value_sum.astype(jnp.bfloat16)
    group_len = tok_rows // group_count
    context = attend(query_rows, key_rows, value_rows, heads_local, group_len)
    live = context[group_len - 1 :]
    live_rows = live.shape[0]
    tensor_count = lax.axis_size("tensor")
    partial_out = jnp.dot(live, w_out, preferred_element_type=jnp.float32).astype(jnp.bfloat16)
    spread = lax.all_to_all(
        partial_out.reshape(live_rows, tensor_count, -1),
        "tensor",
        split_axis=1,
        concat_axis=1,
        tiled=True,
    )
    summed = jnp.sum(spread.astype(jnp.float32), axis=1).astype(jnp.bfloat16)
    return jnp.concatenate([jnp.zeros((group_len - 1, summed.shape[1]), jnp.bfloat16), summed], 0)


def solution(mesh):
    placed = (
        P("dp", "tensor"),
        P("dp", None),
        P("dp", None, "tensor"),
        P(None, "tensor"),
        P(None, "tensor"),
        P(None, "tensor"),
        P("tensor", None),
    )
    return jax.shard_map(
        shards, mesh=mesh, in_specs=placed, out_specs=P("dp", "tensor"), check_vma=False
    )
```

profile of v0, /device:TPU:0, one launch (start us, length us, event | category | flops | bytes accessed | tf_op | source)
XLA Modules:
  0.0 293.9 jit_solution(2541385137041955387)
XLA Ops:
  6.5 0.7 all-gather.5.cloned.1.call-update
  7.3 0.8 copy.33
  8.0 0.1 reshape.302
  8.1 0.2 convert_reduce_fusion
  8.4 0.1 select_reduce_fusion
  8.6 9.5 %all_to_all.19 = s32[8,1,4]{2,1,0:T(1,128)S(1)} all-to-all(s32[8,1,4]{2,1,0:T(1,128)S(1)} %copy.34), channel_id=1, replica_groups=mesh['dp'=8,'tensor'=16] {'dp'}, dimensions={0} | all-to-all | bytes 256 | tf_op jit(solution)/shard_map/all_to_all | solution.py:62
  18.1 0.5 broadcast.311
  18.6 0.7 reduce.4
  19.4 0.1 copy.36
  19.5 5.1 %gather_fusion = bf16[32,128,512]{2,1,0:T(8,128)(2,1)} fusion(bf16[32,128,512]{2,1,0:T(8,128)(2,1)} %param.9, s32[1024]{0:T(1024)S(1)} %pad_clamp_fusion.1), kind=kCustom, calls=%fused_computation | custom fusion | bytes 8388736 | tf_op jit(solution)/shard_map/jit(_take)/gather | solution.py:63
  24.6 4.6 %broadcast_select_fusion = bf16[8,4,128,512]{3,2,1,0:T(8,128)(2,1)} fusion(bf16[8,4,128,512]{3,2,1,0:T(8,128)(2,1)} %bitcast.36, pred[8,4]{1,0:T(8,128)(4,1)S(1)} %copy.36), kind=kLoop, calls=%fused_computation.4 | loop fusion | flops 2097152 | bytes 8388640 | tf_op jit(solution)/shard_map/jit(_take)/select_n | solution.py:63
  29.2 4.6 %all-to-all-start.1 = ((bf16[8,4,128,512]{3,2,1,0:T(8,128)(2,1)}), bf16[8,4,128,512]{3,2,1,0:T(8,128)(2,1)}, u32[]{:S(2)}, u32[]{:S(2)}) async-start(bf16[8,4,128,512]{3,2,1,0:T(8,128)(2,1)} %broadcast_select_fusion), calls=%async_computation.1 | async-start | bytes 8388608 | tf_op jit(solution)/shard_map/all_to_all | solution.py:66
  33.9 49.5 %all-to-all-done.1 = bf16[8,4,128,512]{3,2,1,0:T(8,128)(2,1)} async-done(((bf16[8,4,128,512]{3,2,1,0:T(8,128)(2,1)}), bf16[8,4,128,512]{3,2,1,0:T(8,128)(2,1)}, u32[]{:S(2)}, u32[]{:S(2)}) %all-to-all-start.1) | async-done | bytes 4194336 | tf_op jit(solution)/shard_map/all_to_all | solution.py:66
  83.4 2.8 gather_fusion.1
  86.2 1.1 broadcast_select_fusion.1
  87.4 4.7 %fusion.14 = bf16[256,256]{1,0:T(8,128)(2,1)S(1)} fusion(bf16[256,8192]{1,0:T(8,128)(2,1)} %all-gather.5.cloned.1.call-done, bf16[8192,256]{1,0:T(8,128)(2,1)} %param.10), kind=kOutput, calls=%fused_computation.49 | convolution fusion | flops 1073741824 | bytes 8519680 | tf_op jit(solution)/shard_map/dot_general | solution.py:45
  92.2 115.9 %all-gather.3.cloned.1.call-done = bf16[8,128,8192]{2,1,0:T(8,128)(2,1)} async-done(((bf16[8,128,512]{2,1,0:T(8,128)(2,1)}), bf16[8,128,8192]{2,1,0:T(8,128)(2,1)}) %all-gather.3.cloned.1.call-update) | async-done | bytes 16777232 | tf_op jit(solution)/shard_map/all_gather | solution.py:72
  208.1 11.4 %convolution_convert_fusion.2 = bf16[1024,256]{1,0:T(8,128)(2,1)S(1)} fusion(bf16[1024,8192]{1,0:T(8,128)(2,1)} %bitcast.41, bf16[8192,256]{1,0:T(8,128)(2,1)} %param.12), kind=kOutput, calls=%fused_computation.6 | convolution fusion | flops 4295229440 | bytes 21495808 | tf_op jit(solution)/shard_map/dot_general | solution.py:76
  219.6 0.1 reshape.308
  219.7 11.4 %convolution_convert_fusion.1 = bf16[1024,256]{1,0:T(8,128)(2,1)S(1)} fusion(bf16[1024,8192]{1,0:T(8,128)(2,1)} %bitcast.42, bf16[8192,256]{1,0:T(8,128)(2,1)} %param.11), kind=kOutput, calls=%fused_computation.5 | convolution fusion | flops 4295229440 | bytes 21495808 | tf_op jit(solution)/shard_map/dot_general | solution.py:75
  231.1 0.1 reshape.310
  231.3 0.3 convolution_multiply_fusion
  231.6 0.3 fusion.13
  231.8 1.0 fusion.3
  232.8 0.1 copy.41
  233.0 3.2 %convolution_convert_fusion = bf16[193,8192]{1,0:T(8,128)(2,1)S(1)} fusion(bf16[256,8192]{1,0:T(8,128)(2,1)} %param.13, bf16[256,256]{1,0:T(8,128)(2,1)S(1)} %bitcast.38), kind=kOutput, calls=%fused_computation.3 | convolution fusion | flops 811081728 | bytes 7458816 | tf_op jit(solution)/shard_map/dot_general | solution.py:84
  236.2 1.6 copy.44
  237.8 0.3 slice.14
  238.2 1.8 copy.42
  239.9 45.8 %all_to_all.20 = bf16[193,16,512]{2,0,1:T(8,128)(2,1)S(1)} all-to-all(bf16[193,16,512]{2,0,1:T(8,128)(2,1)S(1)} %copy.42), channel_id=1, replica_groups=mesh['dp'=8,'tensor'=16] {'tensor'}, dimensions={1} | all-to-all | bytes 6324224 | tf_op jit(solution)/shard_map/all_to_all | solution.py:85
  285.7 0.5 reduce_sum.45
  286.3 0.8 concatenate.7
  (21 shorter events, 0.7 us)
Async XLA Ops:
  6.5 80.8 %all-gather.5.cloned.1.call-start = ((), (), s32[]{:S(2)}) async-start(), calls=%async_computation.4 | async-start | bytes 4456448 | tf_op jit(solution)/shard_map/all_gather | solution.py:46
  29.2 54.2 %all-to-all-start.1 = ((bf16[8,4,128,512]{3,2,1,0:T(8,128)(2,1)}), bf16[8,4,128,512]{3,2,1,0:T(8,128)(2,1)}, u32[]{:S(2)}, u32[]{:S(2)}) async-start(bf16[8,4,128,512]{3,2,1,0:T(8,128)(2,1)} %broadcast_select_fusion), calls=%async_computation.1 | async-start | bytes 8388608 | tf_op jit(solution)/shard_map/all_to_all | solution.py:66
  33.7 174.4 %all-gather.3.cloned.1.call-start = ((), (), s32[]{:S(2)}) async-start(), calls=%async_computation.3 | async-start | bytes 17825792 | tf_op jit(solution)/shard_map/all_gather | solution.py:72
Sparse Core Ops, SparseCore 0:
  9.4 59.4 all-gather.4
  87.5 120.6 all-gather.2
where the time goes:
time: 294 us
  waiting for transfers between devices  166 us (56%)
  blocking collectives  55.3 us (19%)
  matrix products  32.1 us (11%)
  local copies, waits for them, and re-layouts  14.6 us (5%)
  between operations  13.6 us (5%)
  other arithmetic  7.61 us (3%)
  starting transfers between devices  4.6 us (2%)
    all_gather x1, waiting for transfers between devices, shards(): lax.all_gather(neighbour_rows, 'tensor', axis=2, tiled=True)  116 us
    all_to_all x1, waiting for transfers between devices, shards(): lax.all_to_all(outgoing, 'dp', split_axis=0, concat_axis=0, tiled=True)  49.5 us
    all_to_all x1, blocking collectives, shards(): lax.all_to_all(partial_out.reshape(live_rows, tensor_count, -1), 'tensor'...  45.8 us
    dot_general x1, matrix products, shards(): value_sum = jnp.dot(assembled, w_value, preferred_element_type=jnp.float32)  11.4 us
    dot_general x1, matrix products, shards(): key_sum = jnp.dot(assembled, w_key, preferred_element_type=jnp.float32)  11.4 us
    all_to_all x1, blocking collectives, shards(): lax.all_to_all(request_table, 'dp', split_axis=0, concat_axis=0, tiled=True)  9.49 us
  transfers between devices with their start and end apart: 3, of which 2 were waited for; matrix products, arithmetic and copies ran while one was open for 7% of the time, Pallas kernels for 0%

commit v1 on v0

--- a/solution.py
+++ b/solution.py
@@ -2,6 +2,7 @@
 import jax.numpy as jnp
 from jax import lax
 from jax.sharding import PartitionSpec as P
+from jax.lax import axis_index, ppermute, psum
 
 HD = 128
 
@@ -69,9 +70,29 @@
         owners * capacity + slot_rank,
         axis=0,
     )
-    assembled = lax.all_gather(neighbour_rows, "tensor", axis=2, tiled=True).reshape(
-        per_reader * ret_len, -1
-    )
+
+    def unite_target(patch):
+        row_axis = "tensor"
+        y2, part_now, built = (psum(1, row_axis), axis_index(row_axis), patch.shape[2])
+        vals = [(src_i, (src_i + 1) % y2) for src_i in range(y2)]
+        lower = jnp.zeros((*patch.shape[:2], y2 * built, *patch.shape[3:]), patch.dtype)
+        lower = lax.dynamic_update_slice_in_dim(lower, patch, part_now * built, axis=2)
+        chunks = [(src_i, (src_i - 1) % y2) for src_i in range(y2)]
+        even = local_now = patch
+        w1 = y2 // 2
+        for to_i in tuple(range(1, w1 + 1)):
+            even = ppermute(even, row_axis, vals)
+            lower = lax.dynamic_update_slice_in_dim(
+                lower, even, (part_now - to_i) % y2 * built, axis=2
+            )
+            if to_i < y2 - w1:
+                local_now = ppermute(local_now, axis_name=row_axis, perm=chunks)
+                lower = lax.dynamic_update_slice_in_dim(
+                    lower, local_now, (part_now + to_i) % y2 * built, axis=2
+                )
+        return lower
+
+    assembled = unite_target(neighbour_rows).reshape(per_reader * ret_len, -1)
     key_sum = jnp.dot(assembled, w_key, preferred_element_type=jnp.float32)
     value_sum = jnp.dot(assembled, w_value, preferred_element_type=jnp.float32)
     key_rows = key_sum.astype(jnp.bfloat16)

time: 294 us -> 372 us (1.27)
  starting transfers between devices: 4.6 us -> 43.2 us
  local copies, waits for them, and re-layouts: 14.6 us -> 50.2 us
  waiting for transfers between devices: 166 us -> 181 us
  blocking collectives: 55.3 us -> 46.9 us
    ppermute x0 -> x15, waiting for transfers between devices: none -> 131 us  [the longest x8 131 us: unite_target(): even = ppermute(even, row_axis, vals)]
    all_gather x1 -> x0, waiting for transfers between devices: 116 us -> none  [shards(): lax.all_gather(neighbour_rows, 'tensor', axis=2, tiled=True)]
    ppermute x0 -> x15, starting transfers between devices: none -> 38.5 us  [the longest x7 37 us: unite_target(): local_now = ppermute(local_now, axis_name=row_axis, perm=chunks)]
    dynamic_update_slice x0 -> x15, local copies, waits for them, and re-layouts: none -> 29.8 us  [the longest x7 15 us: unite_target(): lax.dynamic_update_slice_in_dim(lower, local_now, (part_now + to_i) % y2...]
    all_to_all x1, blocking collectives: 45.8 us -> 37.4 us  [shards(): lax.all_to_all(partial_out.reshape(live_rows, tensor_count, -1), 'tensor'...]
    broadcast_in_dim x0 -> x1, local copies, waits for them, and re-layouts: none -> 6.01 us  [unite_target(): jnp.zeros((*patch.shape[:2], y2 * built, *patch.shape[3:]), patch.dtype)]
  transfers between devices with their start and end apart: 3 -> 17, of which waited for: 2 -> 9; matrix products, arithmetic and copies ran while one was open for 7% -> 12% of each run, Pallas kernels for 0% -> 0%
where the time goes in v1:
time: 372 us; the launch traced here: 371 us
  waiting for transfers between devices  181 us (49%)
  local copies, waits for them, and re-layouts  50.2 us (13%)
  blocking collectives  46.9 us (13%)
  starting transfers between devices  43.2 us (12%)
  matrix products  28.8 us (8%)
  between operations  13.7 us (4%)
  other arithmetic  7.89 us (2%)
    ppermute x8, waiting for transfers between devices, unite_target(): even = ppermute(even, row_axis, vals)  131 us
    all_to_all x1, waiting for transfers between devices, shards(): lax.all_to_all(outgoing, 'dp', split_axis=0, concat_axis=0, tiled=True)  48.8 us
    all_to_all x1, blocking collectives, shards(): lax.all_to_all(partial_out.reshape(live_rows, tensor_count, -1), 'tensor'...  37.4 us
    ppermute x7, starting transfers between devices, unite_target(): local_now = ppermute(local_now, axis_name=row_axis, perm=chunks)  37 us
    dynamic_update_slice x7, local copies, waits for them, and re-layouts, unite_target(): lax.dynamic_update_slice_in_dim(lower, local_now, (part_now + to_i) % y2...  15 us
    dynamic_update_slice x8, local copies, waits for them, and re-layouts, unite_target(): lax.dynamic_update_slice_in_dim(lower, even, (part_now - to_i) % y2 * bui...  14.8 us
    dot_general x1, matrix products, shards(): value_sum = jnp.dot(assembled, w_value, preferred_element_type=jnp.float32)  11.5 us
    all_to_all x1, blocking collectives, shards(): lax.all_to_all(request_table, 'dp', split_axis=0, concat_axis=0, tiled=True)  9.49 us
  transfers between devices with their start and end apart: 17, of which 9 were waited for; matrix products, arithmetic and copies ran while one was open for 12% of the time, Pallas kernels for 0%

profile of v1, /device:TPU:0, one launch (start us, length us, event | category | flops | bytes accessed | tf_op | source)
XLA Modules:
  0.0 371.4 jit_solution(13611403269802943295)
XLA Ops:
  7.8 9.5 %all_to_all.19 = s32[8,1,4]{2,1,0:T(1,128)S(1)} all-to-all(s32[8,1,4]{2,1,0:T(1,128)S(1)} %copy.34), channel_id=1, replica_groups=mesh['dp'=8,'tensor'=16] {'dp'}, dimensions={0} | all-to-all | bytes 256 | tf_op jit(solution)/shard_map/all_to_all | solution.py:63
  18.8 5.0 %gather_fusion = bf16[32,128,512]{2,1,0:T(8,128)(2,1)} fusion(bf16[32,128,512]{2,1,0:T(8,128)(2,1)} %param.9, s32[1024]{0:T(1024)S(1)} %pad_clamp_fusion.1), kind=kCustom, calls=%fused_computation | custom fusion | bytes 8388736 | tf_op jit(solution)/shard_map/jit(_take)/gather | solution.py:64
  23.8 4.6 %broadcast_select_fusion = bf16[8,4,128,512]{3,2,1,0:T(8,128)(2,1)} fusion(bf16[8,4,128,512]{3,2,1,0:T(8,128)(2,1)} %bitcast.36, pred[8,4]{1,0:T(8,128)(4,1)S(1)} %copy.36), kind=kLoop, calls=%fused_computation.4 | loop fusion | flops 2097152 | bytes 8388640 | tf_op jit(solution)/shard_map/jit(_take)/select_n | solution.py:64
  28.4 4.6 %all-to-all-start.1 = ((bf16[8,4,128,512]{3,2,1,0:T(8,128)(2,1)}), bf16[8,4,128,512]{3,2,1,0:T(8,128)(2,1)}, u32[]{:S(2)}, u32[]{:S(2)}) async-start(bf16[8,4,128,512]{3,2,1,0:T(8,128)(2,1)} %broadcast_select_fusion), calls=%async_computation.1 | async-start | bytes 8388608 | tf_op jit(solution)/shard_map/all_to_all | solution.py:67
  33.8 48.8 %all-to-all-done.1 = bf16[8,4,128,512]{3,2,1,0:T(8,128)(2,1)} async-done(((bf16[8,4,128,512]{3,2,1,0:T(8,128)(2,1)}), bf16[8,4,128,512]{3,2,1,0:T(8,128)(2,1)}, u32[]{:S(2)}, u32[]{:S(2)}) %all-to-all-start.1) | async-done | bytes 4194336 | tf_op jit(solution)/shard_map/all_to_all | solution.py:67
  82.6 2.8 gather_fusion.1
  85.4 6.0 %broadcast_in_dim.19 = bf16[8,128,8192]{2,1,0:T(8,128)(2,1)} broadcast(bf16[]{:T(256)} %constant.144.clone.1), dimensions={} | broadcast | bytes 16777218 | tf_op jit(solution)/shard_map/broadcast_in_dim | solution.py:78
  94.4 4.9 %collective-permute-start.1 = (bf16[8,128,512]{2,1,0:T(8,128)(2,1)S(1)}, bf16[8,128,512]{2,1,0:T(8,128)(2,1)S(1)}, u32[]{:S(2)}, u32[]{:S(2)}) collective-permute-start(bf16[8,128,512]{2,1,0:T(8,128)(2,1)S(1)} %get-tuple-element.6), channel_id=1, source_target_pairs={{0,15},{1,0},{2,1},{3,2},{4,3},{5,4},{6,5},{7,6},{8,7},{9,8},{10,9... | collective-permute-start | bytes 3145736 | tf_op jit(solution)/shard_map/ppermute | solution.py:89
  99.3 22.9 %collective-permute-done = bf16[8,128,512]{2,1,0:T(8,128)(2,1)S(1)} collective-permute-done((bf16[8,128,512]{2,1,0:T(8,128)(2,1)S(1)}, bf16[8,128,512]{2,1,0:T(8,128)(2,1)S(1)}, u32[]{:S(2)}, u32[]{:S(2)}) %collective-permute-start) | collective-permute-done | bytes 1048608 | tf_op jit(solution)/shard_map/ppermute | solution.py:84
  122.2 5.3 %collective-permute-start.3 = (bf16[8,128,512]{2,1,0:T(8,128)(2,1)S(1)}, bf16[8,128,512]{2,1,0:T(8,128)(2,1)S(1)}, u32[]{:S(2)}, u32[]{:S(2)}) collective-permute-start(bf16[8,128,512]{2,1,0:T(8,128)(2,1)S(1)} %collective-permute-done.1), channel_id=1, source_target_pairs={{0,15},{1,0},{2,1},{3,2},{4,3},{5,4},{6,5},{7,6},{8,7},{9,8},{10,9... | collective-permute-start | bytes 3145736 | tf_op jit(solution)/shard_map/ppermute | solution.py:89
  127.5 22.0 %collective-permute-done.2 = bf16[8,128,512]{2,1,0:T(8,128)(2,1)S(1)} collective-permute-done((bf16[8,128,512]{2,1,0:T(8,128)(2,1)S(1)}, bf16[8,128,512]{2,1,0:T(8,128)(2,1)S(1)}, u32[]{:S(2)}, u32[]{:S(2)}) %collective-permute-start.2) | collective-permute-done | bytes 1048608 | tf_op jit(solution)/shard_map/ppermute | solution.py:84
  149.5 5.3 %collective-permute-start.5 = (bf16[8,128,512]{2,1,0:T(8,128)(2,1)S(1)}, bf16[8,128,512]{2,1,0:T(8,128)(2,1)S(1)}, u32[]{:S(2)}, u32[]{:S(2)}) collective-permute-start(bf16[8,128,512]{2,1,0:T(8,128)(2,1)S(1)} %collective-permute-done.3), channel_id=1, source_target_pairs={{0,15},{1,0},{2,1},{3,2},{4,3},{5,4},{6,5},{7,6},{8,7},{9,8},{10,9... | collective-permute-start | bytes 3145736 | tf_op jit(solution)/shard_map/ppermute | solution.py:89
  154.9 21.2 %collective-permute-done.4 = bf16[8,128,512]{2,1,0:T(8,128)(2,1)S(1)} collective-permute-done((bf16[8,128,512]{2,1,0:T(8,128)(2,1)S(1)}, bf16[8,128,512]{2,1,0:T(8,128)(2,1)S(1)}, u32[]{:S(2)}, u32[]{:S(2)}) %collective-permute-start.4) | collective-permute-done | bytes 1048608 | tf_op jit(solution)/shard_map/ppermute | solution.py:84
  176.0 5.3 %collective-permute-start.7 = (bf16[8,128,512]{2,1,0:T(8,128)(2,1)S(1)}, bf16[8,128,512]{2,1,0:T(8,128)(2,1)S(1)}, u32[]{:S(2)}, u32[]{:S(2)}) collective-permute-start(bf16[8,128,512]{2,1,0:T(8,128)(2,1)S(1)} %collective-permute-done.5), channel_id=1, source_target_pairs={{0,15},{1,0},{2,1},{3,2},{4,3},{5,4},{6,5},{7,6},{8,7},{9,8},{10,9... | collective-permute-start | bytes 3145736 | tf_op jit(solution)/shard_map/ppermute | solution.py:89
  181.4 20.3 %collective-permute-done.6 = bf16[8,128,512]{2,1,0:T(8,128)(2,1)S(1)} collective-permute-done((bf16[8,128,512]{2,1,0:T(8,128)(2,1)S(1)}, bf16[8,128,512]{2,1,0:T(8,128)(2,1)S(1)}, u32[]{:S(2)}, u32[]{:S(2)}) %collective-permute-start.6) | collective-permute-done | bytes 1048608 | tf_op jit(solution)/shard_map/ppermute | solution.py:84
  201.7 5.3 %collective-permute-start.9 = (bf16[8,128,512]{2,1,0:T(8,128)(2,1)S(1)}, bf16[8,128,512]{2,1,0:T(8,128)(2,1)}, u32[]{:S(2)}, u32[]{:S(2)}) collective-permute-start(bf16[8,128,512]{2,1,0:T(8,128)(2,1)S(1)} %collective-permute-done.7), channel_id=1, source_target_pairs={{0,15},{1,0},{2,1},{3,2},{4,3},{5,4},{6,5},{7,6},{8,7},{9,8},{10,9... | collective-permute-start | bytes 3145736 | tf_op jit(solution)/shard_map/ppermute | solution.py:89
  207.0 19.4 %collective-permute-done.8 = bf16[8,128,512]{2,1,0:T(8,128)(2,1)S(1)} collective-permute-done((bf16[8,128,512]{2,1,0:T(8,128)(2,1)S(1)}, bf16[8,128,512]{2,1,0:T(8,128)(2,1)S(1)}, u32[]{:S(2)}, u32[]{:S(2)}) %collective-permute-start.8) | collective-permute-done | bytes 1048608 | tf_op jit(solution)/shard_map/ppermute | solution.py:84
  226.5 5.4 %collective-permute-start.11 = (bf16[8,128,512]{2,1,0:T(8,128)(2,1)}, bf16[8,128,512]{2,1,0:T(8,128)(2,1)}, u32[]{:S(2)}, u32[]{:S(2)}) collective-permute-start(bf16[8,128,512]{2,1,0:T(8,128)(2,1)} %collective-permute-done.9), channel_id=1, source_target_pairs={{0,15},{1,0},{2,1},{3,2},{4,3},{5,4},{6,5},{7,6},{8,7},{9,8},{10,9... | collective-permute-start | bytes 3145736 | tf_op jit(solution)/shard_map/ppermute | solution.py:89
  231.9 2.3 constant_dynamic-update-slice_fusion.14
  234.3 2.3 constant_dynamic-update-slice_fusion.13
  236.6 13.9 %collective-permute-done.10 = bf16[8,128,512]{2,1,0:T(8,128)(2,1)} collective-permute-done((bf16[8,128,512]{2,1,0:T(8,128)(2,1)S(1)}, bf16[8,128,512]{2,1,0:T(8,128)(2,1)}, u32[]{:S(2)}, u32[]{:S(2)}) %collective-permute-start.10) | collective-permute-done | bytes 1048608 | tf_op jit(solution)/shard_map/ppermute | solution.py:84
  250.5 2.3 constant_dynamic-update-slice_fusion.12
  252.9 2.3 constant_dynamic-update-slice_fusion.11
  257.5 2.3 constant_dynamic-update-slice_fusion.9
  259.8 5.3 %collective-permute-start.13 = (bf16[8,128,512]{2,1,0:T(8,128)(2,1)}, bf16[8,128,512]{2,1,0:T(8,128)(2,1)}, u32[]{:S(2)}, u32[]{:S(2)}) collective-permute-start(bf16[8,128,512]{2,1,0:T(8,128)(2,1)} %collective-permute-done.11), channel_id=1, source_target_pairs={{0,15},{1,0},{2,1},{3,2},{4,3},{5,4},{6,5},{7,6},{8,7},{9,8},{10,9... | collective-permute-start | bytes 3145736 | tf_op jit(solution)/shard_map/ppermute | solution.py:89
  265.1 4.7 %fusion.14 = bf16[256,256]{1,0:T(8,128)(2,1)S(1)} fusion(bf16[256,8192]{1,0:T(8,128)(2,1)} %all-gather.2.cloned.1.call-done, bf16[8192,256]{1,0:T(8,128)(2,1)} %param.10), kind=kOutput, calls=%fused_computation.65 | convolution fusion | flops 1073741824 | bytes 8519680 | tf_op jit(solution)/shard_map/dot_general | solution.py:46
  270.0 4.0 %collective-permute-done.12 = bf16[8,128,512]{2,1,0:T(8,128)(2,1)} collective-permute-done((bf16[8,128,512]{2,1,0:T(8,128)(2,1)}, bf16[8,128,512]{2,1,0:T(8,128)(2,1)}, u32[]{:S(2)}, u32[]{:S(2)}) %collective-permute-start.12) | collective-permute-done | bytes 1048608 | tf_op jit(solution)/shard_map/ppermute | solution.py:84
  288.7 7.6 %collective-permute-done.14 = bf16[8,128,512]{2,1,0:T(8,128)(2,1)S(1)} collective-permute-done((bf16[8,128,512]{2,1,0:T(8,128)(2,1)}, bf16[8,128,512]{2,1,0:T(8,128)(2,1)S(1)}, u32[]{:S(2)}, u32[]{:S(2)}) %collective-permute-start.14) | collective-permute-done | bytes 1048608 | tf_op jit(solution)/shard_map/ppermute | solution.py:84
  297.5 8.2 %convolution_convert_fusion.1 = bf16[1024,256]{1,0:T(8,128)(2,1)S(1)} fusion(bf16[1024,8192]{1,0:T(8,128)(2,1)} %bitcast.7, bf16[8192,256]{1,0:T(8,128)(2,1)S(1)} %copy-done.6), kind=kOutput, calls=%fused_computation.5 | convolution fusion | flops 4295229440 | bytes 21495808 | tf_op jit(solution)/shard_map/dot_general | solution.py:96
  306.4 11.5 %convolution_convert_fusion.2 = bf16[1024,256]{1,0:T(8,128)(2,1)S(1)} fusion(bf16[1024,8192]{1,0:T(8,128)(2,1)} %bitcast.7, bf16[8192,256]{1,0:T(8,128)(2,1)} %param.12), kind=kOutput, calls=%fused_computation.6 | convolution fusion | flops 4295229440 | bytes 21495808 | tf_op jit(solution)/shard_map/dot_general | solution.py:97
  319.1 3.2 convolution_convert_fusion
  325.9 37.4 %all_to_all.20 = bf16[193,16,512]{2,0,1:T(8,128)(2,1)S(1)} all-to-all(bf16[193,16,512]{2,0,1:T(8,128)(2,1)S(1)} %copy.42), channel_id=1, replica_groups=mesh['dp'=8,'tensor'=16] {'tensor'}, dimensions={1} | all-to-all | bytes 6324224 | tf_op jit(solution)/shard_map/all_to_all | solution.py:106
  (78 shorter events, 31.7 us)
Async XLA Ops:
  28.4 54.2 %all-to-all-start.1 = ((bf16[8,4,128,512]{3,2,1,0:T(8,128)(2,1)}), bf16[8,4,128,512]{3,2,1,0:T(8,128)(2,1)}, u32[]{:S(2)}, u32[]{:S(2)}) async-start(bf16[8,4,128,512]{3,2,1,0:T(8,128)(2,1)} %broadcast_select_fusion), calls=%async_computation.1 | async-start | bytes 8388608 | tf_op jit(solution)/shard_map/all_to_all | solution.py:67
  33.0 232.2 %all-gather.2.cloned.1.call-start = ((), (), s32[]{:S(2)}) async-start(), calls=%async_computation.3 | async-start | bytes 4456448 | tf_op jit(solution)/shard_map/all_gather | solution.py:47
  92.8 29.3 %collective-permute-start = (bf16[8,128,512]{2,1,0:T(8,128)(2,1)S(1)}, bf16[8,128,512]{2,1,0:T(8,128)(2,1)S(1)}, u32[]{:S(2)}, u32[]{:S(2)}) collective-permute-start(bf16[8,128,512]{2,1,0:T(8,128)(2,1)S(1)} %get-tuple-element.6), channel_id=1, source_target_pairs={{0,1},{1,2},{2,3},{3,4},{4,5},{5,6},{6,7},{7,8},{8,9},{9,10},{10,1... | collective-permute-start | bytes 3145736 | tf_op jit(solution)/shard_map/ppermute | solution.py:84
  94.4 27.8 %collective-permute-start.1 = (bf16[8,128,512]{2,1,0:T(8,128)(2,1)S(1)}, bf16[8,128,512]{2,1,0:T(8,128)(2,1)S(1)}, u32[]{:S(2)}, u32[]{:S(2)}) collective-permute-start(bf16[8,128,512]{2,1,0:T(8,128)(2,1)S(1)} %get-tuple-element.6), channel_id=1, source_target_pairs={{0,15},{1,0},{2,1},{3,2},{4,3},{5,4},{6,5},{7,6},{8,7},{9,8},{10,9... | collective-permute-start | bytes 3145736 | tf_op jit(solution)/shard_map/ppermute | solution.py:89
  122.1 104.3 %copy-start.1 = (bf16[8,128,512]{2,1,0:T(8,128)(2,1)}, bf16[8,128,512]{2,1,0:T(8,128)(2,1)S(1)}, u32[]{:S(2)}) copy-start(bf16[8,128,512]{2,1,0:T(8,128)(2,1)S(1)} %collective-permute-done) | copy-start | bytes 3145732
  122.2 27.4 %collective-permute-start.2 = (bf16[8,128,512]{2,1,0:T(8,128)(2,1)S(1)}, bf16[8,128,512]{2,1,0:T(8,128)(2,1)S(1)}, u32[]{:S(2)}, u32[]{:S(2)}) collective-permute-start(bf16[8,128,512]{2,1,0:T(8,128)(2,1)S(1)} %collective-permute-done), channel_id=1, source_target_pairs={{0,1},{1,2},{2,3},{3,4},{4,5},{5,6},{6,7},{7,8},{8,9},{9,10},{10,1... | collective-permute-start | bytes 3145736 | tf_op jit(solution)/shard_map/ppermute | solution.py:84
  122.2 104.3 %copy-start.2 = (bf16[8,128,512]{2,1,0:T(8,128)(2,1)}, bf16[8,128,512]{2,1,0:T(8,128)(2,1)S(1)}, u32[]{:S(2)}) copy-start(bf16[8,128,512]{2,1,0:T(8,128)(2,1)S(1)} %collective-permute-done.1) | copy-start | bytes 3145732
  122.2 27.4 %collective-permute-start.3 = (bf16[8,128,512]{2,1,0:T(8,128)(2,1)S(1)}, bf16[8,128,512]{2,1,0:T(8,128)(2,1)S(1)}, u32[]{:S(2)}, u32[]{:S(2)}) collective-permute-start(bf16[8,128,512]{2,1,0:T(8,128)(2,1)S(1)} %collective-permute-done.1), channel_id=1, source_target_pairs={{0,15},{1,0},{2,1},{3,2},{4,3},{5,4},{6,5},{7,6},{8,7},{9,8},{10,9... | collective-permute-start | bytes 3145736 | tf_op jit(solution)/shard_map/ppermute | solution.py:89
  149.5 77.0 %copy-start = (bf16[8,128,512]{2,1,0:T(8,128)(2,1)}, bf16[8,128,512]{2,1,0:T(8,128)(2,1)S(1)}, u32[]{:S(2)}) copy-start(bf16[8,128,512]{2,1,0:T(8,128)(2,1)S(1)} %collective-permute-done.2) | copy-start | bytes 3145732
  149.5 26.5 %collective-permute-start.4 = (bf16[8,128,512]{2,1,0:T(8,128)(2,1)S(1)}, bf16[8,128,512]{2,1,0:T(8,128)(2,1)S(1)}, u32[]{:S(2)}, u32[]{:S(2)}) collective-permute-start(bf16[8,128,512]{2,1,0:T(8,128)(2,1)S(1)} %collective-permute-done.2), channel_id=1, source_target_pairs={{0,1},{1,2},{2,3},{3,4},{4,5},{5,6},{6,7},{7,8},{8,9},{9,10},{10,1... | collective-permute-start | bytes 3145736 | tf_op jit(solution)/shard_map/ppermute | solution.py:84
  149.5 77.0 %copy-start.3 = (bf16[8,128,512]{2,1,0:T(8,128)(2,1)}, bf16[8,128,512]{2,1,0:T(8,128)(2,1)S(1)}, u32[]{:S(2)}) copy-start(bf16[8,128,512]{2,1,0:T(8,128)(2,1)S(1)} %collective-permute-done.3) | copy-start | bytes 3145732
  149.5 26.5 %collective-permute-start.5 = (bf16[8,128,512]{2,1,0:T(8,128)(2,1)S(1)}, bf16[8,128,512]{2,1,0:T(8,128)(2,1)S(1)}, u32[]{:S(2)}, u32[]{:S(2)}) collective-permute-start(bf16[8,128,512]{2,1,0:T(8,128)(2,1)S(1)} %collective-permute-done.3), channel_id=1, source_target_pairs={{0,15},{1,0},{2,1},{3,2},{4,3},{5,4},{6,5},{7,6},{8,7},{9,8},{10,9... | collective-permute-start | bytes 3145736 | tf_op jit(solution)/shard_map/ppermute | solution.py:89
  176.0 50.5 %copy-start.4 = (bf16[8,128,512]{2,1,0:T(8,128)(2,1)}, bf16[8,128,512]{2,1,0:T(8,128)(2,1)S(1)}, u32[]{:S(2)}) copy-start(bf16[8,128,512]{2,1,0:T(8,128)(2,1)S(1)} %collective-permute-done.4) | copy-start | bytes 3145732
  176.0 25.7 %collective-permute-start.6 = (bf16[8,128,512]{2,1,0:T(8,128)(2,1)S(1)}, bf16[8,128,512]{2,1,0:T(8,128)(2,1)S(1)}, u32[]{:S(2)}, u32[]{:S(2)}) collective-permute-start(bf16[8,128,512]{2,1,0:T(8,128)(2,1)S(1)} %collective-permute-done.4), channel_id=1, source_target_pairs={{0,1},{1,2},{2,3},{3,4},{4,5},{5,6},{6,7},{7,8},{8,9},{9,10},{10,1... | collective-permute-start | bytes 3145736 | tf_op jit(solution)/shard_map/ppermute | solution.py:84
  176.0 50.5 %copy-start.5 = (bf16[8,128,512]{2,1,0:T(8,128)(2,1)}, bf16[8,128,512]{2,1,0:T(8,128)(2,1)S(1)}, u32[]{:S(2)}) copy-start(bf16[8,128,512]{2,1,0:T(8,128)(2,1)S(1)} %collective-permute-done.5) | copy-start | bytes 3145732
  176.0 25.6 %collective-permute-start.7 = (bf16[8,128,512]{2,1,0:T(8,128)(2,1)S(1)}, bf16[8,128,512]{2,1,0:T(8,128)(2,1)S(1)}, u32[]{:S(2)}, u32[]{:S(2)}) collective-permute-start(bf16[8,128,512]{2,1,0:T(8,128)(2,1)S(1)} %collective-permute-done.5), channel_id=1, source_target_pairs={{0,15},{1,0},{2,1},{3,2},{4,3},{5,4},{6,5},{7,6},{8,7},{9,8},{10,9... | collective-permute-start | bytes 3145736 | tf_op jit(solution)/shard_map/ppermute | solution.py:89
  201.7 24.8 %collective-permute-start.8 = (bf16[8,128,512]{2,1,0:T(8,128)(2,1)S(1)}, bf16[8,128,512]{2,1,0:T(8,128)(2,1)S(1)}, u32[]{:S(2)}, u32[]{:S(2)}) collective-permute-start(bf16[8,128,512]{2,1,0:T(8,128)(2,1)S(1)} %collective-permute-done.6), channel_id=1, source_target_pairs={{0,1},{1,2},{2,3},{3,4},{4,5},{5,6},{6,7},{7,8},{8,9},{9,10},{10,1... | collective-permute-start | bytes 3145736 | tf_op jit(solution)/shard_map/ppermute | solution.py:84
  201.7 24.8 %collective-permute-start.9 = (bf16[8,128,512]{2,1,0:T(8,128)(2,1)S(1)}, bf16[8,128,512]{2,1,0:T(8,128)(2,1)}, u32[]{:S(2)}, u32[]{:S(2)}) collective-permute-start(bf16[8,128,512]{2,1,0:T(8,128)(2,1)S(1)} %collective-permute-done.7), channel_id=1, source_target_pairs={{0,15},{1,0},{2,1},{3,2},{4,3},{5,4},{6,5},{7,6},{8,7},{9,8},{10,9... | collective-permute-start | bytes 3145736 | tf_op jit(solution)/shard_map/ppermute | solution.py:89
  226.5 24.0 %collective-permute-start.10 = (bf16[8,128,512]{2,1,0:T(8,128)(2,1)S(1)}, bf16[8,128,512]{2,1,0:T(8,128)(2,1)}, u32[]{:S(2)}, u32[]{:S(2)}) collective-permute-start(bf16[8,128,512]{2,1,0:T(8,128)(2,1)S(1)} %collective-permute-done.8), channel_id=1, source_target_pairs={{0,1},{1,2},{2,3},{3,4},{4,5},{5,6},{6,7},{7,8},{8,9},{9,10},{10,1... | collective-permute-start | bytes 3145736 | tf_op jit(solution)/shard_map/ppermute | solution.py:84
  226.5 33.2 %collective-permute-start.11 = (bf16[8,128,512]{2,1,0:T(8,128)(2,1)}, bf16[8,128,512]{2,1,0:T(8,128)(2,1)}, u32[]{:S(2)}, u32[]{:S(2)}) collective-permute-start(bf16[8,128,512]{2,1,0:T(8,128)(2,1)} %collective-permute-done.9), channel_id=1, source_target_pairs={{0,15},{1,0},{2,1},{3,2},{4,3},{5,4},{6,5},{7,6},{8,7},{9,8},{10,9... | collective-permute-start | bytes 3145736 | tf_op jit(solution)/shard_map/ppermute | solution.py:89
  250.5 23.4 %collective-permute-start.12 = (bf16[8,128,512]{2,1,0:T(8,128)(2,1)}, bf16[8,128,512]{2,1,0:T(8,128)(2,1)}, u32[]{:S(2)}, u32[]{:S(2)}) collective-permute-start(bf16[8,128,512]{2,1,0:T(8,128)(2,1)} %collective-permute-done.10), channel_id=1, source_target_pairs={{0,1},{1,2},{2,3},{3,4},{4,5},{5,6},{6,7},{7,8},{8,9},{9,10},{10,1... | collective-permute-start | bytes 3145736 | tf_op jit(solution)/shard_map/ppermute | solution.py:84
  259.8 26.7 %collective-permute-start.13 = (bf16[8,128,512]{2,1,0:T(8,128)(2,1)}, bf16[8,128,512]{2,1,0:T(8,128)(2,1)}, u32[]{:S(2)}, u32[]{:S(2)}) collective-permute-start(bf16[8,128,512]{2,1,0:T(8,128)(2,1)} %collective-permute-done.11), channel_id=1, source_target_pairs={{0,15},{1,0},{2,1},{3,2},{4,3},{5,4},{6,5},{7,6},{8,7},{9,8},{10,9... | collective-permute-start | bytes 3145736 | tf_op jit(solution)/shard_map/ppermute | solution.py:89
  269.9 27.5 %copy-start.6 = (bf16[8192,256]{1,0:T(8,128)(2,1)S(1)}, bf16[8192,256]{1,0:T(8,128)(2,1)}, u32[]{:S(2)}) copy-start(bf16[8192,256]{1,0:T(8,128)(2,1)} %param.11) | copy-start | bytes 12582916
  273.9 22.4 %collective-permute-start.14 = (bf16[8,128,512]{2,1,0:T(8,128)(2,1)}, bf16[8,128,512]{2,1,0:T(8,128)(2,1)S(1)}, u32[]{:S(2)}, u32[]{:S(2)}) collective-permute-start(bf16[8,128,512]{2,1,0:T(8,128)(2,1)} %collective-permute-done.12), channel_id=1, source_target_pairs={{0,1},{1,2},{2,3},{3,4},{4,5},{5,6},{6,7},{7,8},{8,9},{9,10},{10,1... | collective-permute-start | bytes 3145736 | tf_op jit(solution)/shard_map/ppermute | solution.py:84
Sparse Core Ops, SparseCore 0:
  35.9 59.7 all-gather.1
